TPU v7x, 32 devices: a whole 2x2x4 slice. The times are simulated.
32 devices in a mesh: front: 2 (over x), column: 4 (over y, core), row: 4 (over z).
Axes of the slice: x: 2, y: 2, z: 4, core: 2. Of those that a mesh axis runs over, the one named last changes fastest.
Arguments:
- cbs: float32 [2, 2, 2048, 2048], P('front', None, 'row', 'column'), may hold values from -4 to 4
- row_map: int32 [2, 2, 16], P('front'), may hold values from 0 to 47, as said below
- col_map: int32 [2, 2, 16], P('front'), may hold values from 0 to 47, as said below
- child_size: int32 [2, 2], P('front'), may hold values from 8 to 16, as said below
- front_diag: float32 [2, 6144], P('front'), may hold values from 0.1 to 200
- panel_order: int32 [2, 4], P('front'), may hold values from 0 to 23, as said below
- pivot_inverse: float32 [2, 4, 256, 256], P('front'), may hold values from -0.2 to 0.8
Outputs:
- factored_front: float32 [2, 6144, 6144], P('front', 'row', 'column')
Inputs may be any that keep to these rules, and one draw needn't show every extreme that they name: `row_map`: entries of one child are distinct. Split the parent tiles into aligned runs of 12 consecutive tiles (tiles t with the same t // 12, the tiles one row owner holds). In each aligned run of 4 entries at most 2 lie in one such aligned parent run, and in every aligned run of 4 entries some aligned parent run gets exactly 2. `col_map`: entries of one child are distinct. Split the parent tiles into aligned runs of 12 consecutive tiles (tiles t with the same t // 12, the tiles one column owner holds). In each aligned run of 4 entries no two lie in the same such aligned parent run. `child_size`: every front has a child of size 16. `panel_order`: distinct within a front. The first and the last panel block are each eliminated by exactly one front.
All inputs are finite; a program needn't handle non-finite values.
Results may differ from a plain program's by a relative error of at most 0.0003.
Values sent between devices are 32-bit elements; how exact they have to be, the bound alone decides.
No kernel may reach another device: no remote copies, remote signals or barrier semaphores. Data moves between devices by JAX's collectives and lax.ppermute only.
A program may use at most 192 MiB of HBM per device.

v0:
```python
import jax
import jax.numpy as jnp
from jax import lax
from jax.sharding import PartitionSpec as P

ORDER = 6144
TILE = 128
PANEL = 256
PANELS = 4
ROWMOST = 2
HIGHEST = lax.Precision.HIGHEST


def broadcast(block, axis, source):
    block = jnp.where(lax.axis_index(axis) == source, block, jnp.zeros_like(block))
    return lax.psum(block, axis)


def pack_tiles(tile_stack, target_dev, target_spot, dest_count, capacity, sentinel):
    dest_iota = jnp.arange(dest_count, dtype=jnp.int32)
    matches = (target_dev[:, None] == dest_iota[None, :]).astype(jnp.int32)
    earlier = jnp.cumsum(matches, axis=0) - matches
    position = jnp.sum(earlier * matches, axis=1)
    usable = target_dev < dest_count
    slot_index = jnp.where(usable, target_dev * capacity + position, dest_count * capacity)
    payload = jnp.zeros((dest_count * capacity,) + tile_stack.shape[1:], tile_stack.dtype)
    payload = payload.at[slot_index].set(tile_stack, mode="drop")
    labels = (
        jnp.full((dest_count * capacity,), sentinel, jnp.int32)
        .at[slot_index]
        .set(target_spot, mode="drop")
    )
    return (
        payload.reshape((dest_count, capacity) + tile_stack.shape[1:]),
        labels.reshape(dest_count, capacity),
    )


def scatter_tiles(payload, labels, row_tiles, col_tiles):
    tile_side = payload.shape[-1]
    tile_grid = jnp.zeros((row_tiles * col_tiles + 1, tile_side, tile_side), jnp.float32)
    tile_grid = tile_grid.at[labels.reshape(-1)].add(payload.reshape(-1, tile_side, tile_side))
    tile_grid = tile_grid[: row_tiles * col_tiles]
    tile_grid = tile_grid.reshape(row_tiles, col_tiles, tile_side, tile_side).transpose(0, 2, 1, 3)
    return tile_grid.reshape(row_tiles * tile_side, col_tiles * tile_side)


def body(cbs, row_map, col_map, child_size, front_diag, panel_order, pivot_inverse):
    groups = lax.axis_size("front")
    row_devs = lax.axis_size("row")
    col_devs = lax.axis_size("column")
    row_id = lax.axis_index("row")
    col_id = lax.axis_index("column")
    children = cbs.shape[1]
    piece_rows = cbs.shape[2] // TILE
    piece_cols = cbs.shape[3] // TILE
    local_rows = ORDER // row_devs
    local_cols = ORDER // col_devs
    row_tiles = local_rows // TILE
    col_tiles = local_cols // TILE
    sentinel = row_tiles * col_tiles
    tile_stack = (
        cbs[0].reshape(children, piece_rows, TILE, piece_cols, TILE).transpose(0, 1, 3, 2, 4)
    )
    tile_stack = tile_stack.reshape(-1, TILE, TILE)
    child_rows = row_id * piece_rows + jnp.arange(piece_rows, dtype=jnp.int32)
    child_cols = col_id * piece_cols + jnp.arange(piece_cols, dtype=jnp.int32)
    parent_rows = lax.dynamic_slice_in_dim(row_map[0], row_id * piece_rows, piece_rows, 1)
    parent_cols = lax.dynamic_slice_in_dim(col_map[0], col_id * piece_cols, piece_cols, 1)
    live_rows = child_rows[None, :] < child_size[0][:, None]
    live_cols = child_cols[None, :] < child_size[0][:, None]
    owner_rows = parent_rows // row_tiles
    owner_cols = parent_cols // col_tiles
    target_spot = (
        (parent_rows - owner_rows * row_tiles)[:, :, None] * col_tiles
        + (parent_cols - owner_cols * col_tiles)[:, None, :]
    ).reshape(-1)
    usable = (live_rows[:, :, None] & live_cols[:, None, :]).reshape(-1)
    inner_dest = (owner_cols[:, None, :] * row_devs + owner_rows[:, :, None]).reshape(-1)
    all_devices = groups * row_devs * col_devs
    front_ids = jnp.arange(children, dtype=jnp.int32)[:, None]
    whole_dest = (front_ids * (row_devs * col_devs) + inner_dest.reshape(children, -1)).reshape(-1)
    whole_target = jnp.where(usable, whole_dest, all_devices)
    payload, labels = pack_tiles(
        tile_stack, whole_target, target_spot, all_devices, ROWMOST, sentinel
    )
    arrived, arrived_labels = (
        lax.all_to_all(
            payload, ("front", "column", "row"), split_axis=0, concat_axis=0, tiled=True
        ),
        lax.all_to_all(labels, ("front", "column", "row"), split_axis=0, concat_axis=0, tiled=True),
    )
    matrix = scatter_tiles(arrived, arrived_labels, row_tiles, col_tiles)
    row_glob = row_id * local_rows + jnp.arange(local_rows, dtype=jnp.int32)
    col_glob = col_id * local_cols + jnp.arange(local_cols, dtype=jnp.int32)
    diag_part = lax.dynamic_slice_in_dim(front_diag[0], row_id * local_rows, local_rows)
    matrix = matrix + jnp.where(row_glob[:, None] == col_glob[None, :], diag_part[:, None], 0.0)
    order_row = panel_order[0]
    inverses = pivot_inverse[0]
    panel_rows = local_rows // PANEL
    panel_cols = local_cols // PANEL
    row_block = row_glob // PANEL
    col_block = col_glob // PANEL

    def strip_bounds(step_index):
        pivot_block = order_row[step_index]
        return (
            pivot_block // panel_cols,
            pivot_block // panel_rows,
            pivot_block % panel_cols * PANEL,
            pivot_block % panel_rows * PANEL,
        )

    def actives(step_index):
        chosen = order_row[: step_index + 1]
        active_rows = jnp.all(row_block[:, None] != chosen[None, :], axis=1)
        active_cols = jnp.all(col_block[:, None] != chosen[None, :], axis=1)
        return (active_rows, active_cols)

    def current_strips(matrix, step_index):
        col_owner, row_owner, col_offset, row_offset = strip_bounds(step_index)
        return (
            lax.dynamic_slice_in_dim(matrix, col_offset, PANEL, 1),
            lax.dynamic_slice_in_dim(matrix, row_offset, PANEL, 0),
        )

    def share_strips(col_strip, row_strip, step_index):
        col_owner, row_owner, col_offset, row_offset = strip_bounds(step_index)
        owner_left = jnp.dot(
            col_strip, inverses[step_index], precision=HIGHEST, preferred_element_type=jnp.float32
        )
        left_strip = broadcast(owner_left, "column", col_owner)
        top_strip = broadcast(row_strip, "row", row_owner)
        return (left_strip, top_strip)

    first_col, first_row = current_strips(matrix, 0)
    left_strip, top_strip = share_strips(first_col, first_row, 0)
    for step_index in range(PANELS):
        if step_index + 1 < PANELS:
            active_rows, active_cols = actives(step_index)
            next_col, next_row = current_strips(matrix, step_index + 1)
            col_owner, row_owner, col_offset, row_offset = strip_bounds(step_index + 1)
            top_part = lax.dynamic_slice_in_dim(top_strip, col_offset, PANEL, 1)
            left_part = lax.dynamic_slice_in_dim(left_strip, row_offset, PANEL, 0)
            next_col = jnp.where(
                active_rows[:, None],
                next_col
                - jnp.dot(
                    left_strip, top_part, precision=HIGHEST, preferred_element_type=jnp.float32
                ),
                next_col,
            )
            next_row = jnp.where(
                active_cols[None, :],
                next_row
                - jnp.dot(
                    left_part, top_strip, precision=HIGHEST, preferred_element_type=jnp.float32
                ),
                next_row,
            )
            left_next, top_next = share_strips(next_col, next_row, step_index + 1)
        eliminate_matrix = matrix
        eliminate_active_rows, eliminate_active_cols = actives(step_index)
        product = jnp.dot(
            left_strip, top_strip, precision=HIGHEST, preferred_element_type=jnp.float32
        )
        eliminate_matrix = jnp.where(
            eliminate_active_rows[:, None] & eliminate_active_cols[None, :],
            eliminate_matrix - product,
            eliminate_matrix,
        )
        eliminate_col_owner, eliminate_row_owner, eliminate_col_offset, eliminate_row_offset = (
            strip_bounds(step_index)
        )
        present = lax.dynamic_slice_in_dim(eliminate_matrix, eliminate_col_offset, PANEL, 1)
        fresh_col = jnp.where(
            (col_id == eliminate_col_owner) & eliminate_active_rows[:, None], left_strip, present
        )
        matrix = lax.dynamic_update_slice_in_dim(
            eliminate_matrix, fresh_col, eliminate_col_offset, 1
        )
        if step_index + 1 < PANELS:
            left_strip, top_strip = (left_next, top_next)
    return matrix[None]


def solution(mesh):
    placed = (
        P("front", None, "row", "column"),
        P("front", None, None),
        P("front", None, None),
        P("front", None),
        P("front", None),
        P("front", None),
        P("front", None, None, None),
    )
    return jax.shard_map(
        body, mesh=mesh, in_specs=placed, out_specs=P("front", "row", "column"), check_vma=False
    )
```

profile of v0, /device:TPU:0, one launch (start us, length us, event | category | flops | bytes accessed | tf_op | source)
XLA Modules:
  0.0 678.1 jit_solution(4158527166542845537)
XLA Ops:
  6.5 0.7 broadcast_compare_fusion.3
  7.8 0.8 multiply_subtract_fusion
  10.0 0.7 all_to_all.9
  10.7 7.3 %all-to-all-start = ((s32[32,1,2]{2,1,0:T(1,128)}), s32[32,1,2]{2,1,0:T(1,128)S(1)}, u32[]{:S(2)}, u32[]{:S(2)}) async-start(s32[32,1,2]{2,1,0:T(1,128)} %bitcast.9), calls=%async_computation | async-start | bytes 32768 | tf_op jit(solution)/shard_map/all_to_all | solution.py:91
  18.0 2.9 reshape_squeeze.3
  20.9 1.9 copy.15
  22.8 2.5 broadcast_in_dim.159
  25.3 5.3 scatter_fusion
  30.7 5.8 all-to-all-start.1
  39.8 0.7 reduce.5
  40.6 86.3 %all-to-all-done.1 = f32[32,2,128,128]{3,2,1,0:T(8,128)} async-done(((f32[32,2,128,128]{3,2,1,0:T(8,128)}), f32[32,2,128,128]{3,2,1,0:T(8,128)}, u32[]{:S(2)}, u32[]{:S(2)}) %all-to-all-start.1) | async-done | bytes 4194336 | tf_op jit(solution)/shard_map/all_to_all | solution.py:88
  127.0 4.8 broadcast_in_dim.154
  131.8 14.1 %scatter_fusion.1 = f32[145,128,128]{2,1,0:T(8,128)} fusion(f32[145,128,128]{2,1,0:T(8,128)} %broadcast_in_dim.154, s32[64]{0:T(128)S(1)} %fusion.41, f32[64,128,128]{2,1,0:T(8,128)} %bitcast.14), kind=kCustom, calls=%fused_computation.2 | custom fusion | flops 1048576 | bytes 12583168 | tf_op jit(solution)/shard_map/scatter-add | solution.py:42
  145.9 8.8 %slice.69 = f32[144,128,128]{2,1,0:T(8,128)} slice(f32[145,128,128]{2,1,0:T(8,128)} %scatter_fusion.1), slice={[0:144], [0:128], [0:128]} | slice | bytes 18874368 | tf_op jit(solution)/shard_map/slice | solution.py:43
  154.7 9.9 %copy.16 = f32[12,128,12,128]{3,2,1,0:T(8,128)S(1)} copy(f32[12,128,12,128]{3,1,2,0:T(8,128)} %bitcast.90) | data formatting | bytes 18874368 | tf_op jit(solution)/shard_map/transpose | solution.py:44
  164.7 3.1 bitcast_add_fusion
  167.8 3.7 copy-done.2
  171.5 3.7 convolution_select_fusion.3
  175.3 2.7 dynamic-slice_select_fusion
  180.3 39.8 %all-reduce.9.cloned.1.call-done = f32[1536,256]{1,0:T(8,128)} async-done(((f32[1536,256]{1,0:T(8,128)}), f32[1536,256]{1,0:T(8,128)}) %all-reduce.9.cloned.1.call-update) | async-done | bytes 1572880 | tf_op jit(solution)/shard_map/psum | solution.py:16
  220.2 71.6 %all-reduce.11.cloned.1.call-done = f32[256,1536]{1,0:T(8,128)} async-done(((f32[256,1536]{1,0:T(8,128)}), f32[256,1536]{1,0:T(8,128)}) %all-reduce.11.cloned.1.call-update) | async-done | bytes 1572880 | tf_op jit(solution)/shard_map/psum | solution.py:16
  291.7 3.4 fusion.8
  295.2 3.6 convolution_select_fusion.2
  298.9 0.8 broadcast_compare_fusion
  300.2 4.1 fusion.7
  307.2 12.5 %subtract_select_fusion.3 = f32[1536,1536]{1,0:T(8,128)} fusion(f32[1536,1536]{1,0:T(8,128)} %copy-done.2, f32[1536,256]{1,0:T(8,128)S(1)} %copy-done.4, f32[256,1536]{1,0:T(8,128)S(1)} %copy-done.7, pred[1536]{0:T(1024)(128)(4,1)S(1)} %broadcast_compare_fusion, pred[1536]{0:T(1024)(128)(4,1)S(1)} %broadcast_compare_fusion.1), kind=kOutput, calls=%fused_computation.6 | convolution fusion | flops 7254835200 | bytes 22023168 | tf_op jit(solution)/shard_map/dot_general | solution.py:164
  319.7 2.9 select_dynamic-update-slice_fusion.2
  322.6 18.2 %all-reduce.13.cloned.1.call-done = f32[1536,256]{1,0:T(8,128)} async-done(((f32[1536,256]{1,0:T(8,128)}), f32[1536,256]{1,0:T(8,128)}) %all-reduce.13.cloned.1.call-update) | async-done | bytes 1572880 | tf_op jit(solution)/shard_map/psum | solution.py:16
  340.9 71.4 %all-reduce.15.cloned.1.call-done = f32[256,1536]{1,0:T(8,128)} async-done(((f32[256,1536]{1,0:T(8,128)}), f32[256,1536]{1,0:T(8,128)}) %all-reduce.15.cloned.1.call-update) | async-done | bytes 1572880 | tf_op jit(solution)/shard_map/psum | solution.py:16
  412.3 3.4 fusion.5
  415.7 3.6 convolution_select_fusion.1
  419.6 1.1 copy-done.3
  420.7 4.1 fusion.4
  426.7 12.5 %subtract_select_fusion.2 = f32[1536,1536]{1,0:T(8,128)} fusion(f32[1536,1536]{1,0:T(8,128)} %select_dynamic-update-slice_fusion.2, f32[1536,256]{1,0:T(8,128)S(1)} %copy-done.3, f32[256,1536]{1,0:T(8,128)S(1)} %copy-done.6, pred[1536]{0:T(1024)(128)(4,1)S(1)} %get-tuple-element.10, pred[1536]{0:T(1024)(128)(4,1)S(1)} %get-tuple-element.9), kind=kOutput, calls=%fused_computation.5 | convolution fusion | flops 7254835200 | bytes 22023168 | tf_op jit(solution)/shard_map/dot_general | solution.py:164
  439.2 2.9 select_dynamic-update-slice_fusion.1
  442.2 19.3 %all-reduce.17.cloned.1.call-done = f32[1536,256]{1,0:T(8,128)} async-done(((f32[1536,256]{1,0:T(8,128)}), f32[1536,256]{1,0:T(8,128)}) %all-reduce.17.cloned.1.call-update) | async-done | bytes 1572880 | tf_op jit(solution)/shard_map/psum | solution.py:16
  461.4 71.4 %all-reduce.19.cloned.1.call-done = f32[256,1536]{1,0:T(8,128)} async-done(((f32[256,1536]{1,0:T(8,128)}), f32[256,1536]{1,0:T(8,128)}) %all-reduce.19.cloned.1.call-update) | async-done | bytes 1572880 | tf_op jit(solution)/shard_map/psum | solution.py:16
  532.8 3.4 fusion.2
  536.3 3.6 convolution_select_fusion
  540.3 1.1 copy-done.5
  541.3 4.1 fusion.1
  545.6 12.5 %subtract_select_fusion.1 = f32[1536,1536]{1,0:T(8,128)} fusion(f32[1536,1536]{1,0:T(8,128)} %select_dynamic-update-slice_fusion.1, f32[1536,256]{1,0:T(8,128)S(1)} %copy-done.5, f32[256,1536]{1,0:T(8,128)S(1)} %copy-done.8, pred[1536]{0:T(1024)(128)(4,1)S(1)} %get-tuple-element.8, pred[1536]{0:T(1024)(128)(4,1)S(1)} %get-tuple-element.7), kind=kOutput, calls=%fused_computation.4 | convolution fusion | flops 7254835200 | bytes 22023168 | tf_op jit(solution)/shard_map/dot_general | solution.py:164
  558.0 2.9 select_dynamic-update-slice_fusion
  561.0 21.0 %all-reduce.21.cloned.1.call-done = f32[1536,256]{1,0:T(8,128)} async-done(((f32[1536,256]{1,0:T(8,128)}), f32[1536,256]{1,0:T(8,128)}) %all-reduce.21.cloned.1.call-update) | async-done | bytes 1572880 | tf_op jit(solution)/shard_map/psum | solution.py:16
  582.0 71.6 %all-reduce.23.cloned.1.call-done = f32[256,1536]{1,0:T(8,128)} async-done(((f32[256,1536]{1,0:T(8,128)}), f32[256,1536]{1,0:T(8,128)}) %all-reduce.23.cloned.1.call-update) | async-done | bytes 1572880 | tf_op jit(solution)/shard_map/psum | solution.py:16
  653.6 12.2 %subtract_select_fusion = f32[1536,1536]{1,0:T(8,128)S(1)} fusion(f32[1536,1536]{1,0:T(8,128)} %select_dynamic-update-slice_fusion, f32[1536,256]{1,0:T(8,128)} %all-reduce.21.cloned.1.call-done, f32[256,1536]{1,0:T(8,128)} %all-reduce.23.cloned.1.call-done, pred[1536]{0:T(1024)(128)(4,1)S(1)} %get-tuple-element.6, pred[1536]{0:T(1024)(128)(4,1)S(1)} %get-tuple-element.5), kind=kOutput, calls=%fused_computation.3 | convolution fusion | flops 7254835200 | bytes 22023168 | tf_op jit(solution)/shard_map/dot_general | solution.py:164
  665.9 3.7 copy.32
  669.6 1.4 bitcast_dynamic-update-slice_fusion
  (74 shorter events, 6.5 us)
Async XLA Ops:
  6.5 32.6 %copy-start = (f32[1,6144]{1,0:T(1,128)S(1)}, f32[1,6144]{1,0:T(1,128)}, u32[]{:S(2)}) copy-start(f32[1,6144]{1,0:T(1,128)} %param.11) | copy-start | bytes 73732
  10.7 19.9 %all-to-all-start = ((s32[32,1,2]{2,1,0:T(1,128)}), s32[32,1,2]{2,1,0:T(1,128)S(1)}, u32[]{:S(2)}, u32[]{:S(2)}) async-start(s32[32,1,2]{2,1,0:T(1,128)} %bitcast.9), calls=%async_computation | async-start | bytes 32768 | tf_op jit(solution)/shard_map/all_to_all | solution.py:91
  30.7 5.9 copy-start.10
  30.7 96.3 %all-to-all-start.1 = ((f32[32,2,128,128]{3,2,1,0:T(8,128)}), f32[32,2,128,128]{3,2,1,0:T(8,128)}, u32[]{:S(2)}, u32[]{:S(2)}) async-start(f32[32,2,128,128]{3,2,1,0:T(8,128)} %bitcast.91), calls=%async_computation.1 | async-start | bytes 8388608 | tf_op jit(solution)/shard_map/all_to_all | solution.py:88
  36.5 183.7 %all-reduce.9.cloned.1.call-start = ((), (), s32[]{:S(2)}) async-start(), calls=%async_computation.2 | async-start | bytes 3145728 | tf_op jit(solution)/shard_map/psum | solution.py:16
  167.8 3.7 copy-start.2
  175.2 116.5 %all-reduce.11.cloned.1.call-start = ((), (), s32[]{:S(2)}) async-start(), calls=%async_computation.3 | async-start | bytes 3145728 | tf_op jit(solution)/shard_map/psum | solution.py:16
  178.0 162.9 %all-reduce.13.cloned.1.call-start = ((), (), s32[]{:S(2)}) async-start(), calls=%async_computation.4 | async-start | bytes 3145728 | tf_op jit(solution)/shard_map/psum | solution.py:16
  295.2 4.5 copy-start.7
  298.8 1.4 copy-start.4
  298.8 113.5 %all-reduce.15.cloned.1.call-start = ((), (), s32[]{:S(2)}) async-start(), calls=%async_computation.5 | async-start | bytes 3145728 | tf_op jit(solution)/shard_map/psum | solution.py:16
  304.3 157.1 %all-reduce.17.cloned.1.call-start = ((), (), s32[]{:S(2)}) async-start(), calls=%async_computation.6 | async-start | bytes 3145728 | tf_op jit(solution)/shard_map/psum | solution.py:16
  415.7 3.9 copy-start.6
  419.3 1.4 copy-start.3
  419.4 113.5 %all-reduce.19.cloned.1.call-start = ((), (), s32[]{:S(2)}) async-start(), calls=%async_computation.7 | async-start | bytes 3145728 | tf_op jit(solution)/shard_map/psum | solution.py:16
  424.9 157.1 %all-reduce.21.cloned.1.call-start = ((), (), s32[]{:S(2)}) async-start(), calls=%async_computation.8 | async-start | bytes 3145728 | tf_op jit(solution)/shard_map/psum | solution.py:16
  536.3 4.0 copy-start.8
  539.9 1.4 copy-start.5
  539.9 113.6 %all-reduce.23.cloned.1.call-start = ((), (), s32[]{:S(2)}) async-start(), calls=%async_computation.9 | async-start | bytes 3145728 | tf_op jit(solution)/shard_map/psum | solution.py:16
  665.8 3.8 copy-start.9
  665.8 5.2 copy-start.1
Sparse Core Ops, SparseCore 0:
  175.3 44.7 all-reduce.8
  222.5 69.1 all-reduce.10
  298.9 41.8 all-reduce.12
  343.1 69.1 all-reduce.14
  419.5 41.8 all-reduce.16
  463.6 69.1 all-reduce.18
  540.1 41.8 all-reduce.20
  584.4 69.1 all-reduce.22
where the time goes:
time: 683 us; the launch traced here: 678 us
  waiting for transfers between devices  471 us (69%)
  matrix products  86.7 us (13%)
  local copies, waits for them, and re-layouts  49.8 us (7%)
  other arithmetic  35.4 us (5%)
  between operations  21.5 us (3%)
  starting transfers between devices  13.9 us (2%)
    psum x8, waiting for transfers between devices, broadcast(): return lax.psum(block, axis)  384 us
    all_to_all x1, waiting for transfers between devices, body(): lax.all_to_all(payload, ('front', 'column', 'row'), split_axis=0, concat_...  86.3 us
    dot_general x4, matrix products, body(): jnp.dot(left_strip, top_strip, precision=HIGHEST, preferred_element_type=...  49.7 us
    dot_general x4, matrix products, share_strips(): jnp.dot(col_strip, inverses[step_index], precision=HIGHEST, preferred_ele...  14.5 us
    scatter-add x1, other arithmetic, scatter_tiles(): tile_grid.at[labels.reshape(-1)]  14.1 us
  transfers between devices with their start and end apart: 10, of which 9 were waited for; matrix products, arithmetic and copies ran while one was open for 12% of the time, Pallas kernels for 0%

commit v1 on v0

--- a/solution.py
+++ b/solution.py
@@ -13,7 +13,7 @@
 
 def broadcast(block, axis, source):
     block = jnp.where(lax.axis_index(axis) == source, block, jnp.zeros_like(block))
-    return lax.psum(block, axis)
+    return jnp.sum(lax.all_gather(block, axis_name=axis), axis=0)
 
 
 def pack_tiles(tile_stack, target_dev, target_spot, dest_count, capacity, sentinel):

time: 683 us -> 876 us (1.28)
  waiting for transfers between devices: 471 us -> 641 us
  other arithmetic: 35.4 us -> 62.2 us
    all_gather x0 -> x8, waiting for transfers between devices: none -> 554 us  [broadcast(): return jnp.sum(lax.all_gather(block, axis_name=axis), axis=0)]
    psum x8 -> x0, waiting for transfers between devices: 384 us -> none  [broadcast(): return lax.psum(block, axis)]
    reduce_sum x0 -> x8, other arithmetic: none -> 28.4 us  [broadcast(): return jnp.sum(lax.all_gather(block, axis_name=axis), axis=0)]
where the time goes in v1:
time: 876 us; the launch traced here: 872 us
  waiting for transfers between devices  641 us (73%)
  matrix products  85.6 us (10%)
  other arithmetic  62.2 us (7%)
  local copies, waits for them, and re-layouts  47 us (5%)
  between operations  21.8 us (2%)
  starting transfers between devices  14.1 us (2%)
    all_gather x8, waiting for transfers between devices, broadcast(): return jnp.sum(lax.all_gather(block, axis_name=axis), axis=0)  554 us
    all_to_all x1, waiting for transfers between devices, body(): lax.all_to_all(payload, ('front', 'column', 'row'), split_axis=0, concat_...  86.6 us
    dot_general x4, matrix products, body(): jnp.dot(left_strip, top_strip, precision=HIGHEST, preferred_element_type=...  50.1 us
    reduce_sum x8, other arithmetic, broadcast(): return jnp.sum(lax.all_gather(block, axis_name=axis), axis=0)  28.4 us
  transfers between devices with their start and end apart: 10, of which 9 were waited for; matrix products, arithmetic and copies ran while one was open for 12% of the time, Pallas kernels for 0%

profile of v1, /device:TPU:0, one launch (start us, length us, event | category | flops | bytes accessed | tf_op | source)
XLA Modules:
  0.0 871.8 jit_solution(8531724899407355998)
XLA Ops:
  10.7 7.3 all-to-all-start
  18.0 2.9 reshape_squeeze.3
  20.9 1.9 copy.15
  22.8 2.5 broadcast_in_dim.159
  25.3 5.3 scatter_fusion
  30.7 5.8 all-to-all-start.1
  40.4 86.6 %all-to-all-done.1 = f32[32,2,128,128]{3,2,1,0:T(8,128)} async-done(((f32[32,2,128,128]{3,2,1,0:T(8,128)}), f32[32,2,128,128]{3,2,1,0:T(8,128)}, u32[]{:S(2)}, u32[]{:S(2)}) %all-to-all-start.1) | async-done | bytes 4194336 | tf_op jit(solution)/shard_map/all_to_all | solution.py:88
  127.0 4.8 broadcast_in_dim.154
  131.8 14.2 %scatter_fusion.1 = f32[145,128,128]{2,1,0:T(8,128)} fusion(f32[145,128,128]{2,1,0:T(8,128)} %broadcast_in_dim.154, s32[64]{0:T(128)S(1)} %fusion.41, f32[64,128,128]{2,1,0:T(8,128)} %bitcast.14), kind=kCustom, calls=%fused_computation.2 | custom fusion | flops 1048576 | bytes 12583168 | tf_op jit(solution)/shard_map/scatter-add | solution.py:42
  146.0 8.8 %slice.69 = f32[144,128,128]{2,1,0:T(8,128)} slice(f32[145,128,128]{2,1,0:T(8,128)} %scatter_fusion.1), slice={[0:144], [0:128], [0:128]} | slice | bytes 18874368 | tf_op jit(solution)/shard_map/slice | solution.py:43
  154.8 9.9 %copy.16 = f32[12,128,12,128]{3,2,1,0:T(8,128)S(1)} copy(f32[12,128,12,128]{3,1,2,0:T(8,128)} %bitcast.98) | data formatting | bytes 18874368 | tf_op jit(solution)/shard_map/transpose | solution.py:44
  164.7 3.1 bitcast_add_fusion
  167.9 3.7 copy-done.2
  173.1 4.0 convolution_select_fusion.3
  179.7 110.6 %all-gather.19.cloned.1.call-done = f32[1024,1536]{1,0:T(8,128)} async-done(((f32[256,1536]{1,0:T(8,128)}), f32[1024,1536]{1,0:T(8,128)}) %all-gather.19.cloned.1.call-update) | async-done | bytes 6291472 | tf_op jit(solution)/shard_map/all_gather | solution.py:16
  290.3 3.6 reduce_sum.86
  293.9 42.6 %all-gather.17.cloned.1.call-done = f32[6144,256]{1,0:T(8,128)} async-done(((f32[1536,256]{1,0:T(8,128)}), f32[6144,256]{1,0:T(8,128)}) %all-gather.17.cloned.1.call-update) | async-done | bytes 6291472 | tf_op jit(solution)/shard_map/all_gather | solution.py:16
  336.5 3.5 reduce_sum.85
  340.0 4.1 fusion.7
  344.8 2.9 fusion.8
  347.7 3.5 convolution_select_fusion.2
  354.1 12.8 %subtract_select_fusion.3 = f32[1536,1536]{1,0:T(8,128)} fusion(f32[1536,1536]{1,0:T(8,128)} %copy-done.2, f32[1536,256]{1,0:T(8,128)S(1)} %reduce_sum.85, f32[256,1536]{1,0:T(8,128)S(1)} %reduce_sum.86, pred[1536]{0:T(1024)(128)(4,1)S(1)} %broadcast_compare_fusion, pred[1536]{0:T(1024)(128)(4,1)S(1)} %broadcast_compare_fusion.1), kind=kOutput, calls=%fused_computation.6 | convolution fusion | flops 7254835200 | bytes 22023168 | tf_op jit(solution)/shard_map/dot_general | solution.py:164
  366.9 2.9 select_dynamic-update-slice_fusion.2
  369.8 89.8 %all-gather.23.cloned.1.call-done = f32[1024,1536]{1,0:T(8,128)} async-done(((f32[256,1536]{1,0:T(8,128)}), f32[1024,1536]{1,0:T(8,128)}) %all-gather.23.cloned.1.call-update) | async-done | bytes 6291472 | tf_op jit(solution)/shard_map/all_gather | solution.py:16
  459.6 3.6 reduce_sum.88
  463.3 42.4 %all-gather.21.cloned.1.call-done = f32[6144,256]{1,0:T(8,128)} async-done(((f32[1536,256]{1,0:T(8,128)}), f32[6144,256]{1,0:T(8,128)}) %all-gather.21.cloned.1.call-update) | async-done | bytes 6291472 | tf_op jit(solution)/shard_map/all_gather | solution.py:16
  505.7 3.5 reduce_sum.87
  509.2 4.1 fusion.4
  513.4 2.9 fusion.5
  516.2 3.6 convolution_select_fusion.1
  522.2 12.6 %subtract_select_fusion.2 = f32[1536,1536]{1,0:T(8,128)} fusion(f32[1536,1536]{1,0:T(8,128)} %select_dynamic-update-slice_fusion.2, f32[1536,256]{1,0:T(8,128)S(1)} %reduce_sum.87, f32[256,1536]{1,0:T(8,128)S(1)} %reduce_sum.88, pred[1536]{0:T(1024)(128)(4,1)S(1)} %get-tuple-element.10, pred[1536]{0:T(1024)(128)(4,1)S(1)} %get-tuple-element.9), kind=kOutput, calls=%fused_computation.5 | convolution fusion | flops 7254835200 | bytes 22023168 | tf_op jit(solution)/shard_map/dot_general | solution.py:164
  534.8 2.9 select_dynamic-update-slice_fusion.1
  537.8 91.1 %all-gather.27.cloned.1.call-done = f32[1024,1536]{1,0:T(8,128)} async-done(((f32[256,1536]{1,0:T(8,128)}), f32[1024,1536]{1,0:T(8,128)}) %all-gather.27.cloned.1.call-update) | async-done | bytes 6291472 | tf_op jit(solution)/shard_map/all_gather | solution.py:16
  628.8 3.6 reduce_sum.90
  632.4 42.5 %all-gather.25.cloned.1.call-done = f32[6144,256]{1,0:T(8,128)} async-done(((f32[1536,256]{1,0:T(8,128)}), f32[6144,256]{1,0:T(8,128)}) %all-gather.25.cloned.1.call-update) | async-done | bytes 6291472 | tf_op jit(solution)/shard_map/all_gather | solution.py:16
  674.9 3.5 reduce_sum.89
  678.4 4.1 fusion.1
  682.5 2.9 fusion.2
  685.4 3.6 convolution_select_fusion
  689.1 13.2 %subtract_select_fusion.1 = f32[1536,1536]{1,0:T(8,128)} fusion(f32[1536,1536]{1,0:T(8,128)} %select_dynamic-update-slice_fusion.1, f32[1536,256]{1,0:T(8,128)S(1)} %reduce_sum.89, f32[256,1536]{1,0:T(8,128)S(1)} %reduce_sum.90, pred[1536]{0:T(1024)(128)(4,1)S(1)} %get-tuple-element.8, pred[1536]{0:T(1024)(128)(4,1)S(1)} %get-tuple-element.7), kind=kOutput, calls=%fused_computation.4 | convolution fusion | flops 7254835200 | bytes 22023168 | tf_op jit(solution)/shard_map/dot_general | solution.py:164
  702.3 2.9 select_dynamic-update-slice_fusion
  705.2 92.8 %all-gather.31.cloned.1.call-done = f32[1024,1536]{1,0:T(8,128)} async-done(((f32[256,1536]{1,0:T(8,128)}), f32[1024,1536]{1,0:T(8,128)}) %all-gather.31.cloned.1.call-update) | async-done | bytes 6291472 | tf_op jit(solution)/shard_map/all_gather | solution.py:16
  798.0 3.6 reduce_sum.92
  801.6 42.6 %all-gather.29.cloned.1.call-done = f32[6144,256]{1,0:T(8,128)} async-done(((f32[1536,256]{1,0:T(8,128)}), f32[6144,256]{1,0:T(8,128)}) %all-gather.29.cloned.1.call-update) | async-done | bytes 6291472 | tf_op jit(solution)/shard_map/all_gather | solution.py:16
  844.2 3.5 reduce_sum.91
  847.7 11.5 %subtract_select_fusion = f32[1536,1536]{1,0:T(8,128)S(1)} fusion(f32[1536,1536]{1,0:T(8,128)} %select_dynamic-update-slice_fusion, f32[1536,256]{1,0:T(8,128)S(1)} %reduce_sum.91, f32[256,1536]{1,0:T(8,128)S(1)} %reduce_sum.92, pred[1536]{0:T(1024)(128)(4,1)S(1)} %get-tuple-element.6, pred[1536]{0:T(1024)(128)(4,1)S(1)} %get-tuple-element.5), kind=kOutput, calls=%fused_computation.3 | convolution fusion | flops 7254835200 | bytes 22023168 | tf_op jit(solution)/shard_map/dot_general | solution.py:164
  859.3 3.7 copy.24
  863.0 1.4 bitcast_dynamic-update-slice_fusion
  (68 shorter events, 10.7 us)
Async XLA Ops:
  6.5 32.6 %copy-start = (f32[1,6144]{1,0:T(1,128)S(1)}, f32[1,6144]{1,0:T(1,128)}, u32[]{:S(2)}) copy-start(f32[1,6144]{1,0:T(1,128)} %param.11) | copy-start | bytes 73732
  10.7 19.9 %all-to-all-start = ((s32[32,1,2]{2,1,0:T(1,128)}), s32[32,1,2]{2,1,0:T(1,128)S(1)}, u32[]{:S(2)}, u32[]{:S(2)}) async-start(s32[32,1,2]{2,1,0:T(1,128)} %bitcast.9), calls=%async_computation | async-start | bytes 32768 | tf_op jit(solution)/shard_map/all_to_all | solution.py:91
  30.7 5.9 copy-start.3
  30.7 96.3 %all-to-all-start.1 = ((f32[32,2,128,128]{3,2,1,0:T(8,128)}), f32[32,2,128,128]{3,2,1,0:T(8,128)}, u32[]{:S(2)}, u32[]{:S(2)}) async-start(f32[32,2,128,128]{3,2,1,0:T(8,128)} %bitcast.99), calls=%async_computation.1 | async-start | bytes 8388608 | tf_op jit(solution)/shard_map/all_to_all | solution.py:88
  36.5 253.9 %all-gather.19.cloned.1.call-start = ((), (), s32[]{:S(2)}) async-start(), calls=%async_computation.3 | async-start | bytes 7864320 | tf_op jit(solution)/shard_map/all_gather | solution.py:16
  167.9 3.7 copy-start.2
  172.9 163.6 %all-gather.17.cloned.1.call-start = ((), (), s32[]{:S(2)}) async-start(), calls=%async_computation.2 | async-start | bytes 7864320 | tf_op jit(solution)/shard_map/all_gather | solution.py:16
  177.2 282.5 %all-gather.23.cloned.1.call-start = ((), (), s32[]{:S(2)}) async-start(), calls=%async_computation.5 | async-start | bytes 7864320 | tf_op jit(solution)/shard_map/all_gather | solution.py:16
  344.1 161.6 %all-gather.21.cloned.1.call-start = ((), (), s32[]{:S(2)}) async-start(), calls=%async_computation.4 | async-start | bytes 7864320 | tf_op jit(solution)/shard_map/all_gather | solution.py:16
  351.3 277.5 %all-gather.27.cloned.1.call-start = ((), (), s32[]{:S(2)}) async-start(), calls=%async_computation.7 | async-start | bytes 7864320 | tf_op jit(solution)/shard_map/all_gather | solution.py:16
  513.3 161.6 %all-gather.25.cloned.1.call-start = ((), (), s32[]{:S(2)}) async-start(), calls=%async_computation.6 | async-start | bytes 7864320 | tf_op jit(solution)/shard_map/all_gather | solution.py:16
  519.8 278.2 %all-gather.31.cloned.1.call-start = ((), (), s32[]{:S(2)}) async-start(), calls=%async_computation.9 | async-start | bytes 7864320 | tf_op jit(solution)/shard_map/all_gather | solution.py:16
  682.5 161.7 %all-gather.29.cloned.1.call-start = ((), (), s32[]{:S(2)}) async-start(), calls=%async_computation.8 | async-start | bytes 7864320 | tf_op jit(solution)/shard_map/all_gather | solution.py:16
  859.2 5.2 copy-start.1
Sparse Core Ops, SparseCore 0:
  173.0 117.2 all-gather.18
  291.9 44.5 all-gather.16
  344.3 115.3 all-gather.22
  461.1 44.5 all-gather.20
  513.4 115.3 all-gather.26
  630.2 44.5 all-gather.24
  682.6 115.3 all-gather.30
  799.6 44.5 all-gather.28
